TPU v7x, 32 devices: a whole 2x2x4 slice. The times are simulated.
32 devices in a mesh: tensor: 4 (over x, core), replica: 4 (over z), fsdp: 2 (over y).
Axes of the slice: x: 2, y: 2, z: 4, core: 2. Of those that a mesh axis runs over, the one named last changes fastest.
Arguments:
- gradients: bfloat16 [4, 128, 28672], P('replica', 'fsdp', 'tensor'), may hold values from -6 to 6
- seeds: int32 [2], replicated, may hold values from 0 to 1073741823
- adam_step: int32 [1], replicated, may hold values from 1 to 8
- first_moment: float32 [128, 28672], P(('fsdp', 'replica'), 'tensor'), may hold values from -0.6 to 0.6
- second_moment: float32 [128, 28672], P(('fsdp', 'replica'), 'tensor'), may hold values from 0.001 to 0.1
Outputs:
- new_first: float32 [128, 28672], P(('fsdp', 'replica'), 'tensor')
- new_second: float32 [128, 28672], P(('fsdp', 'replica'), 'tensor')
- step_update: float32 [128, 28672], P(('fsdp', 'replica'), 'tensor')
All inputs are finite; a program needn't handle non-finite values.
Results may differ from a plain program's by a relative error of at most 0.012.
The roundings to bfloat16 on the way count: a program that leaves them out, or rounds other values in their place, can miss the bound.
Values may be sent and summed in bfloat16 or wider, within the bound.
No kernel may reach another device: no remote copies, remote signals or barrier semaphores. Data moves between devices by JAX's collectives and lax.ppermute only.
A program may use at most 64 MiB of HBM per device.

v0:
```python
import math
import jax
import jax.numpy as jnp
from jax import lax
from jax.sharding import PartitionSpec as P

RANK = 512


def scramble(value):
    value = value ^ lax.shift_right_logical(value, jnp.full_like(value, 16))
    value = value * jnp.int32(-2048144789)
    value = value ^ lax.shift_right_logical(value, jnp.full_like(value, 13))
    value = value * jnp.int32(-1028477387)
    value = value ^ lax.shift_right_logical(value, jnp.full_like(value, 16))
    return value


def projection_block(first_column, columns, rank, seeds):
    seed_key = seeds[0] ^ seeds[1] * jnp.int32(668265263)
    column = lax.broadcasted_iota(jnp.int32, (columns, rank), 0) + first_column
    entry = lax.broadcasted_iota(jnp.int32, (columns, rank), 1)
    counter = (column * jnp.int32(rank) + entry) * jnp.int32(2)
    hash_a = scramble(counter * jnp.int32(-1640531535) ^ seed_key)
    hash_b = scramble((counter + jnp.int32(1)) * jnp.int32(-1640531535) ^ seed_key)
    inverse = 1.0 / 16777216.0
    uniform_a = (
        lax.shift_right_logical(hash_a, jnp.full_like(hash_a, 8)).astype(jnp.float32) + 0.5
    ) * inverse
    uniform_b = (
        lax.shift_right_logical(hash_b, jnp.full_like(hash_b, 8)).astype(jnp.float32) + 0.5
    ) * inverse
    gauss = jnp.sqrt(-2.0 * jnp.log(uniform_a)) * jnp.cos(6.283185307179586 * uniform_b)
    return (gauss * rank ** (-0.5)).astype(jnp.bfloat16)


def per_device(gradients, seeds, adam_step, first_moment, second_moment):
    gradient = gradients[0]
    columns = gradient.shape[1]
    replicas = lax.axis_size("replica")
    column_start = lax.axis_index("tensor") * jnp.int32(columns)
    piece_cols = math.gcd(columns, 512)
    blocks = columns // piece_cols
    starts = column_start + lax.iota(jnp.int32, blocks) * jnp.int32(piece_cols)
    tiles = lax.map(lambda first: projection_block(first, piece_cols, RANK, seeds), starts)
    projection = tiles.reshape(columns, RANK)
    partial_value = jnp.dot(gradient, projection, preferred_element_type=jnp.float32) * (
        1.0 / replicas
    )
    share = lax.psum_scatter(partial_value, "replica", scatter_dimension=0, tiled=True)
    sketch = lax.psum(share, "tensor")
    sketch_rounded = sketch.astype(jnp.bfloat16)
    estimate = lax.dot_general(
        sketch_rounded, projection, (((1,), (1,)), ((), ())), preferred_element_type=jnp.float32
    )
    new_first = 0.9 * first_moment + 0.1 * estimate
    new_second = 0.95 * second_moment + 0.05 * estimate * estimate
    step_float = adam_step[0].astype(jnp.float32)
    fix_first = 1.0 - jnp.power(jnp.float32(0.9), step_float)
    fix_second = 1.0 - jnp.power(jnp.float32(0.95), step_float)
    step_update = new_first / fix_first / (jnp.sqrt(new_second / fix_second) + 1e-08)
    return (new_first, new_second, step_update)


def solution(mesh):
    placed = (
        P("replica", "fsdp", "tensor"),
        P(),
        P(),
        P(("fsdp", "replica"), "tensor"),
        P(("fsdp", "replica"), "tensor"),
    )
    return jax.shard_map(
        per_device,
        mesh=mesh,
        in_specs=placed,
        out_specs=(
            P(("fsdp", "replica"), "tensor"),
            P(("fsdp", "replica"), "tensor"),
            P(("fsdp", "replica"), "tensor"),
        ),
        check_vma=False,
    )
```

profile of v0, /device:TPU:1, one launch (start us, length us, event | category | flops | bytes accessed | tf_op | source)
XLA Modules:
  0.0 164.6 jit_solution(9987295474891056560)
XLA Ops:
  7.2 1.3 fusion.26
  9.9 99.4 %while.12 = (s32[]{:T(128)}, bf16[14,512,512]{2,1,0:T(8,128)(2,1)}, s32[14]{0:T(128)S(1)}, s32[]{:T(128)}, s32[]{:T(128)}) while((s32[]{:T(128)}, bf16[14,512,512]{2,1,0:T(8,128)(2,1)}, s32[14]{0:T(128)S(1)}, s32[]{:T(128)}, s32[]{:T(128)}) %tuple.33), condition=%wide.region_1.2_spmd, body=%wide.region_0.1_spmd.sunk | while | flops 9176066 | bytes 529485 | solution.py:45
  11.1 5.9 %fusion.31 = bf16[14,512,512]{2,1,0:T(8,128)(2,1)} fusion(bf16[14,512,512]{2,1,0:T(8,128)(2,1)} %get-tuple-element.105, s32[]{:T(128)} %get-tuple-element.104, s32[]{:T(128)} %get-tuple-element.112, s32[512]{0:T(512)S(1)} %add_multiply_fusion.2), kind=kLoop, calls=%fused_computation.25.clone.1 | loop fusion | flops 9175040 | bytes 527360 | tf_op jit(solution)/shard_map/while/body/jit(dynamic_update_index_in_dim)/dynamic_update_slice | solution.py:45
  17.6 0.6 add_multiply_fusion.2
  18.2 5.9 %fusion.31 = bf16[14,512,512]{2,1,0:T(8,128)(2,1)} fusion(bf16[14,512,512]{2,1,0:T(8,128)(2,1)} %get-tuple-element.105, s32[]{:T(128)} %get-tuple-element.104, s32[]{:T(128)} %get-tuple-element.112, s32[512]{0:T(512)S(1)} %add_multiply_fusion.2), kind=kLoop, calls=%fused_computation.25.clone.1 | loop fusion | flops 9175040 | bytes 527360 | tf_op jit(solution)/shard_map/while/body/jit(dynamic_update_index_in_dim)/dynamic_update_slice | solution.py:45
  25.3 5.9 %fusion.31 = bf16[14,512,512]{2,1,0:T(8,128)(2,1)} fusion(bf16[14,512,512]{2,1,0:T(8,128)(2,1)} %get-tuple-element.105, s32[]{:T(128)} %get-tuple-element.104, s32[]{:T(128)} %get-tuple-element.112, s32[512]{0:T(512)S(1)} %add_multiply_fusion.2), kind=kLoop, calls=%fused_computation.25.clone.1 | loop fusion | flops 9175040 | bytes 527360 | tf_op jit(solution)/shard_map/while/body/jit(dynamic_update_index_in_dim)/dynamic_update_slice | solution.py:45
  31.8 0.6 add_multiply_fusion.2
  32.4 5.9 %fusion.31 = bf16[14,512,512]{2,1,0:T(8,128)(2,1)} fusion(bf16[14,512,512]{2,1,0:T(8,128)(2,1)} %get-tuple-element.105, s32[]{:T(128)} %get-tuple-element.104, s32[]{:T(128)} %get-tuple-element.112, s32[512]{0:T(512)S(1)} %add_multiply_fusion.2), kind=kLoop, calls=%fused_computation.25.clone.1 | loop fusion | flops 9175040 | bytes 527360 | tf_op jit(solution)/shard_map/while/body/jit(dynamic_update_index_in_dim)/dynamic_update_slice | solution.py:45
  38.9 0.6 add_multiply_fusion.2
  39.5 5.8 %fusion.31 = bf16[14,512,512]{2,1,0:T(8,128)(2,1)} fusion(bf16[14,512,512]{2,1,0:T(8,128)(2,1)} %get-tuple-element.105, s32[]{:T(128)} %get-tuple-element.104, s32[]{:T(128)} %get-tuple-element.112, s32[512]{0:T(512)S(1)} %add_multiply_fusion.2), kind=kLoop, calls=%fused_computation.25.clone.1 | loop fusion | flops 9175040 | bytes 527360 | tf_op jit(solution)/shard_map/while/body/jit(dynamic_update_index_in_dim)/dynamic_update_slice | solution.py:45
  46.0 0.6 add_multiply_fusion.2
  46.6 5.9 %fusion.31 = bf16[14,512,512]{2,1,0:T(8,128)(2,1)} fusion(bf16[14,512,512]{2,1,0:T(8,128)(2,1)} %get-tuple-element.105, s32[]{:T(128)} %get-tuple-element.104, s32[]{:T(128)} %get-tuple-element.112, s32[512]{0:T(512)S(1)} %add_multiply_fusion.2), kind=kLoop, calls=%fused_computation.25.clone.1 | loop fusion | flops 9175040 | bytes 527360 | tf_op jit(solution)/shard_map/while/body/jit(dynamic_update_index_in_dim)/dynamic_update_slice | solution.py:45
  53.0 0.6 add_multiply_fusion.2
  53.7 5.9 %fusion.31 = bf16[14,512,512]{2,1,0:T(8,128)(2,1)} fusion(bf16[14,512,512]{2,1,0:T(8,128)(2,1)} %get-tuple-element.105, s32[]{:T(128)} %get-tuple-element.104, s32[]{:T(128)} %get-tuple-element.112, s32[512]{0:T(512)S(1)} %add_multiply_fusion.2), kind=kLoop, calls=%fused_computation.25.clone.1 | loop fusion | flops 9175040 | bytes 527360 | tf_op jit(solution)/shard_map/while/body/jit(dynamic_update_index_in_dim)/dynamic_update_slice | solution.py:45
  60.1 0.6 add_multiply_fusion.2
  60.8 5.9 %fusion.31 = bf16[14,512,512]{2,1,0:T(8,128)(2,1)} fusion(bf16[14,512,512]{2,1,0:T(8,128)(2,1)} %get-tuple-element.105, s32[]{:T(128)} %get-tuple-element.104, s32[]{:T(128)} %get-tuple-element.112, s32[512]{0:T(512)S(1)} %add_multiply_fusion.2), kind=kLoop, calls=%fused_computation.25.clone.1 | loop fusion | flops 9175040 | bytes 527360 | tf_op jit(solution)/shard_map/while/body/jit(dynamic_update_index_in_dim)/dynamic_update_slice | solution.py:45
  67.2 0.6 add_multiply_fusion.2
  67.9 5.9 %fusion.31 = bf16[14,512,512]{2,1,0:T(8,128)(2,1)} fusion(bf16[14,512,512]{2,1,0:T(8,128)(2,1)} %get-tuple-element.105, s32[]{:T(128)} %get-tuple-element.104, s32[]{:T(128)} %get-tuple-element.112, s32[512]{0:T(512)S(1)} %add_multiply_fusion.2), kind=kLoop, calls=%fused_computation.25.clone.1 | loop fusion | flops 9175040 | bytes 527360 | tf_op jit(solution)/shard_map/while/body/jit(dynamic_update_index_in_dim)/dynamic_update_slice | solution.py:45
  74.3 0.6 add_multiply_fusion.2
  75.0 5.9 %fusion.31 = bf16[14,512,512]{2,1,0:T(8,128)(2,1)} fusion(bf16[14,512,512]{2,1,0:T(8,128)(2,1)} %get-tuple-element.105, s32[]{:T(128)} %get-tuple-element.104, s32[]{:T(128)} %get-tuple-element.112, s32[512]{0:T(512)S(1)} %add_multiply_fusion.2), kind=kLoop, calls=%fused_computation.25.clone.1 | loop fusion | flops 9175040 | bytes 527360 | tf_op jit(solution)/shard_map/while/body/jit(dynamic_update_index_in_dim)/dynamic_update_slice | solution.py:45
  82.1 5.9 %fusion.31 = bf16[14,512,512]{2,1,0:T(8,128)(2,1)} fusion(bf16[14,512,512]{2,1,0:T(8,128)(2,1)} %get-tuple-element.105, s32[]{:T(128)} %get-tuple-element.104, s32[]{:T(128)} %get-tuple-element.112, s32[512]{0:T(512)S(1)} %add_multiply_fusion.2), kind=kLoop, calls=%fused_computation.25.clone.1 | loop fusion | flops 9175040 | bytes 527360 | tf_op jit(solution)/shard_map/while/body/jit(dynamic_update_index_in_dim)/dynamic_update_slice | solution.py:45
  88.5 0.6 add_multiply_fusion.2
  89.2 5.9 %fusion.31 = bf16[14,512,512]{2,1,0:T(8,128)(2,1)} fusion(bf16[14,512,512]{2,1,0:T(8,128)(2,1)} %get-tuple-element.105, s32[]{:T(128)} %get-tuple-element.104, s32[]{:T(128)} %get-tuple-element.112, s32[512]{0:T(512)S(1)} %add_multiply_fusion.2), kind=kLoop, calls=%fused_computation.25.clone.1 | loop fusion | flops 9175040 | bytes 527360 | tf_op jit(solution)/shard_map/while/body/jit(dynamic_update_index_in_dim)/dynamic_update_slice | solution.py:45
  95.6 0.6 add_multiply_fusion.2
  96.3 5.9 %fusion.31 = bf16[14,512,512]{2,1,0:T(8,128)(2,1)} fusion(bf16[14,512,512]{2,1,0:T(8,128)(2,1)} %get-tuple-element.105, s32[]{:T(128)} %get-tuple-element.104, s32[]{:T(128)} %get-tuple-element.112, s32[512]{0:T(512)S(1)} %add_multiply_fusion.2), kind=kLoop, calls=%fused_computation.25.clone.1 | loop fusion | flops 9175040 | bytes 527360 | tf_op jit(solution)/shard_map/while/body/jit(dynamic_update_index_in_dim)/dynamic_update_slice | solution.py:45
  103.4 5.9 %fusion.31 = bf16[14,512,512]{2,1,0:T(8,128)(2,1)} fusion(bf16[14,512,512]{2,1,0:T(8,128)(2,1)} %get-tuple-element.105, s32[]{:T(128)} %get-tuple-element.104, s32[]{:T(128)} %get-tuple-element.112, s32[512]{0:T(512)S(1)} %add_multiply_fusion.2), kind=kLoop, calls=%fused_computation.25.clone.1 | loop fusion | flops 9175040 | bytes 527360 | tf_op jit(solution)/shard_map/while/body/jit(dynamic_update_index_in_dim)/dynamic_update_slice | solution.py:45
  109.2 5.2 %fusion.20 = f32[64,512]{0,1:T(8,128)S(1)} fusion(bf16[7168,512]{1,0:T(8,128)(2,1)} %bitcast.16, bf16[1,64,7168]{2,1,0:T(8,128)(2,1)S(1)} %copy-done), kind=kOutput, calls=%fused_computation.28 | convolution fusion | flops 469794816 | bytes 8388608 | tf_op jit(solution)/shard_map/dot_general | solution.py:47
  114.4 0.8 copy.8
  116.0 18.6 %reduce-scatter.4.cloned.1.call-done = f32[16,512]{1,0:T(8,128)} async-done(((f32[64,512]{1,0:T(8,128)}), f32[16,512]{1,0:T(8,128)}) %reduce-scatter.4.cloned.1.call-update) | async-done | bytes 32784
  134.5 0.9 copy.9
  135.4 16.2 %psum.7 = bf16[16,512]{0,1:T(8,128)(2,1)S(1)} all-reduce(f32[16,512]{0,1:T(8,128)S(1)} %copy.9), channel_id=1, replica_groups=mesh['tensor'=4,'replica'=4,'fsdp'=2] {'tensor'}, use_global_device_ids=true, to_apply=%region_3.4 | all-reduce | flops 8192 | bytes 49152 | tf_op jit(solution)/shard_map/psum | solution.py:51
  151.6 6.2 %multiply_divide_fusion = (f32[16,7168]{1,0:T(8,128)}, f32[16,7168]{1,0:T(8,128)}, f32[16,7168]{1,0:T(8,128)}) fusion(f32[]{:T(128)} %bitcast.6, f32[]{:T(128)} %bitcast.5, f32[16,7168]{1,0:T(8,128)S(1)} %copy-done.1, f32[16,7168]{1,0:T(8,128)S(1)} %copy-done.2, bf16[16,512]{0,1:T(8,128)(2,1)S(1)} %psum.7, bf16[7168,512]{1,0:T(8,128)(2,1)} %bitcast.17), kind=kOutput, calls=%fused_computation.32 | convolution fusion | flops 118702080 | bytes 9650184 | tf_op jit(solution)/shard_map/dot_general | solution.py:53
  (28 shorter events, 10.8 us)
Async XLA Ops:
  7.2 102.1 %copy-start = (bf16[1,64,7168]{2,1,0:T(8,128)(2,1)S(1)}, bf16[1,64,7168]{2,1,0:T(8,128)(2,1)}, u32[]{:S(2)}) copy-start(bf16[1,64,7168]{2,1,0:T(8,128)(2,1)} %param.7) | copy-start | bytes 2752516
  7.2 127.3 %reduce-scatter.4.cloned.1.call-start = ((), (), s32[]{:S(2)}) async-start(), calls=%async_computation.1 | async-start | bytes 163840
  9.9 141.7 %copy-start.1 = (f32[16,7168]{1,0:T(8,128)S(1)}, f32[16,7168]{1,0:T(8,128)}, u32[]{:S(2)}) copy-start(f32[16,7168]{1,0:T(8,128)} %param.11) | copy-start | bytes 1376260
  9.9 141.7 %copy-start.2 = (f32[16,7168]{1,0:T(8,128)S(1)}, f32[16,7168]{1,0:T(8,128)}, u32[]{:S(2)}) copy-start(f32[16,7168]{1,0:T(8,128)} %param.10) | copy-start | bytes 1376260
Sparse Core Ops, SparseCore 0:
  115.3 19.1 reduce-scatter.3
where the time goes:
time: 165 us
  other arithmetic  91.1 us (55%)
  waiting for transfers between devices  18.6 us (11%)
  blocking collectives  16.2 us (10%)
  between operations  16.1 us (10%)
  matrix products  11.4 us (7%)
  local copies, waits for them, and re-layouts  11.2 us (7%)
    dynamic_update_slice x14, other arithmetic, per_device(): lax.map(lambda first: projection_block(first, piece_cols, RANK, seeds), s...  82 us
    unnamed x2, waiting for transfers between devices  18.6 us
    psum x1, blocking collectives, per_device(): sketch = lax.psum(share, 'tensor')  16.2 us
    mul x14, other arithmetic, projection_block(): counter = (column * jnp.int32(rank) + entry) * jnp.int32(2)  9.07 us
    dynamic_slice x14, local copies, waits for them, and re-layouts, per_device(): lax.map(lambda first: projection_block(first, piece_cols, RANK, seeds), s...  8.15 us
    dot_general x1, matrix products, per_device(): lax.dot_general(sketch_rounded, projection, (((1,), (1,)), ((), ())), pre...  6.19 us
    dot_general x1, matrix products, per_device(): jnp.dot(gradient, projection, preferred_element_type=jnp.float32)  5.17 us
  transfers between devices with their start and end apart: 1, of which 1 were waited for; matrix products, arithmetic and copies ran while one was open for 0% of the time, Pallas kernels for 0%

commit v1 on v0

--- a/solution.py
+++ b/solution.py
@@ -48,7 +48,10 @@
         1.0 / replicas
     )
     share = lax.psum_scatter(partial_value, "replica", scatter_dimension=0, tiled=True)
-    sketch = lax.psum(share, "tensor")
+    devices, sketch = (lax.axis_size("tensor"), share)
+    for hop in [1 << k for k in range(devices.bit_length() - 1)]:
+        pairs = [(i, i ^ hop) for i in range(devices)]
+        sketch = sketch + lax.ppermute(sketch, "tensor", pairs)
     sketch_rounded = sketch.astype(jnp.bfloat16)
     estimate = lax.dot_general(
         sketch_rounded, projection, (((1,), (1,)), ((), ())), preferred_element_type=jnp.float32

time: 165 us -> 156 us (0.945)
  blocking collectives: 16.2 us -> 0 us
  starting transfers between devices: 0.04 us -> 4.25 us
  waiting for transfers between devices: 18.6 us -> 21.2 us
  local copies, waits for them, and re-layouts: 11.2 us -> 9.49 us
    reduce_scatter x0 -> x1, waiting for transfers between devices: none -> 19.3 us  [per_device(): lax.psum_scatter(partial_value, 'replica', scatter_dimension=0, tiled=True)]
    unnamed x2 -> x1, waiting for transfers between devices: 18.6 us -> 0.02 us
    psum x1 -> x0, blocking collectives: 16.2 us -> none  [per_device(): sketch = lax.psum(share, 'tensor')]
    ppermute x0 -> x2, starting transfers between devices: none -> 4.22 us  [per_device(): sketch = sketch + lax.ppermute(sketch, 'tensor', pairs)]
    ppermute x0 -> x2, waiting for transfers between devices: none -> 1.93 us  [per_device(): sketch = sketch + lax.ppermute(sketch, 'tensor', pairs)]
    unnamed x8 -> x6, local copies, waits for them, and re-layouts: 1.67 us -> 0.02 us
  transfers between devices with their start and end apart: 1 -> 3, of which waited for: 1 -> 3; matrix products, arithmetic and copies ran while one was open for 0% -> 0% of each run, Pallas kernels for 0% -> 0%
where the time goes in v1:
time: 156 us; the launch traced here: 154 us
  other arithmetic  91.9 us (59%)
  waiting for transfers between devices  21.2 us (14%)
  between operations  16.1 us (10%)
  matrix products  11.4 us (7%)
  local copies, waits for them, and re-layouts  9.49 us (6%)
  starting transfers between devices  4.25 us (3%)
    dynamic_update_slice x14, other arithmetic, per_device(): lax.map(lambda first: projection_block(first, piece_cols, RANK, seeds), s...  82.1 us
    reduce_scatter x1, waiting for transfers between devices, per_device(): lax.psum_scatter(partial_value, 'replica', scatter_dimension=0, tiled=True)  19.3 us
    mul x14, other arithmetic, projection_block(): counter = (column * jnp.int32(rank) + entry) * jnp.int32(2)  9.07 us
    dynamic_slice x14, local copies, waits for them, and re-layouts, per_device(): lax.map(lambda first: projection_block(first, piece_cols, RANK, seeds), s...  8.15 us
    dot_general x1, matrix products, per_device(): lax.dot_general(sketch_rounded, projection, (((1,), (1,)), ((), ())), pre...  6.18 us
    dot_general x1, matrix products, per_device(): jnp.dot(gradient, projection, preferred_element_type=jnp.float32)  5.2 us
    ppermute x2, starting transfers between devices, per_device(): sketch = sketch + lax.ppermute(sketch, 'tensor', pairs)  4.22 us
  transfers between devices with their start and end apart: 3, of which 3 were waited for; matrix products, arithmetic and copies ran while one was open for 0% of the time, Pallas kernels for 0%

profile of v1, /device:TPU:1, one launch (start us, length us, event | category | flops | bytes accessed | tf_op | source)
XLA Modules:
  0.0 154.5 jit_solution(4229950016771891826)
XLA Ops:
  7.2 1.3 fusion.25
  9.9 99.4 %while.12 = (s32[]{:T(128)}, bf16[14,512,512]{2,1,0:T(8,128)(2,1)}, s32[14]{0:T(128)S(1)}, s32[]{:T(128)}, s32[]{:T(128)}) while((s32[]{:T(128)}, bf16[14,512,512]{2,1,0:T(8,128)(2,1)}, s32[14]{0:T(128)S(1)}, s32[]{:T(128)}, s32[]{:T(128)}) %tuple.33), condition=%wide.region_1.2_spmd, body=%wide.region_0.1_spmd.sunk | while | flops 9176066 | bytes 529485 | solution.py:45
  10.5 0.6 add_multiply_fusion.2
  11.1 5.9 %fusion.29 = bf16[14,512,512]{2,1,0:T(8,128)(2,1)} fusion(bf16[14,512,512]{2,1,0:T(8,128)(2,1)} %get-tuple-element.105, s32[]{:T(128)} %get-tuple-element.104, s32[]{:T(128)} %get-tuple-element.112, s32[512]{0:T(512)S(1)} %add_multiply_fusion.2), kind=kLoop, calls=%fused_computation.25.clone.1 | loop fusion | flops 9175040 | bytes 527360 | tf_op jit(solution)/shard_map/while/body/jit(dynamic_update_index_in_dim)/dynamic_update_slice | solution.py:45
  17.6 0.6 add_multiply_fusion.2
  18.2 5.9 %fusion.29 = bf16[14,512,512]{2,1,0:T(8,128)(2,1)} fusion(bf16[14,512,512]{2,1,0:T(8,128)(2,1)} %get-tuple-element.105, s32[]{:T(128)} %get-tuple-element.104, s32[]{:T(128)} %get-tuple-element.112, s32[512]{0:T(512)S(1)} %add_multiply_fusion.2), kind=kLoop, calls=%fused_computation.25.clone.1 | loop fusion | flops 9175040 | bytes 527360 | tf_op jit(solution)/shard_map/while/body/jit(dynamic_update_index_in_dim)/dynamic_update_slice | solution.py:45
  25.3 5.9 %fusion.29 = bf16[14,512,512]{2,1,0:T(8,128)(2,1)} fusion(bf16[14,512,512]{2,1,0:T(8,128)(2,1)} %get-tuple-element.105, s32[]{:T(128)} %get-tuple-element.104, s32[]{:T(128)} %get-tuple-element.112, s32[512]{0:T(512)S(1)} %add_multiply_fusion.2), kind=kLoop, calls=%fused_computation.25.clone.1 | loop fusion | flops 9175040 | bytes 527360 | tf_op jit(solution)/shard_map/while/body/jit(dynamic_update_index_in_dim)/dynamic_update_slice | solution.py:45
  31.8 0.6 add_multiply_fusion.2
  32.4 5.9 %fusion.29 = bf16[14,512,512]{2,1,0:T(8,128)(2,1)} fusion(bf16[14,512,512]{2,1,0:T(8,128)(2,1)} %get-tuple-element.105, s32[]{:T(128)} %get-tuple-element.104, s32[]{:T(128)} %get-tuple-element.112, s32[512]{0:T(512)S(1)} %add_multiply_fusion.2), kind=kLoop, calls=%fused_computation.25.clone.1 | loop fusion | flops 9175040 | bytes 527360 | tf_op jit(solution)/shard_map/while/body/jit(dynamic_update_index_in_dim)/dynamic_update_slice | solution.py:45
  38.9 0.6 add_multiply_fusion.2
  39.5 5.9 %fusion.29 = bf16[14,512,512]{2,1,0:T(8,128)(2,1)} fusion(bf16[14,512,512]{2,1,0:T(8,128)(2,1)} %get-tuple-element.105, s32[]{:T(128)} %get-tuple-element.104, s32[]{:T(128)} %get-tuple-element.112, s32[512]{0:T(512)S(1)} %add_multiply_fusion.2), kind=kLoop, calls=%fused_computation.25.clone.1 | loop fusion | flops 9175040 | bytes 527360 | tf_op jit(solution)/shard_map/while/body/jit(dynamic_update_index_in_dim)/dynamic_update_slice | solution.py:45
  46.6 5.9 %fusion.29 = bf16[14,512,512]{2,1,0:T(8,128)(2,1)} fusion(bf16[14,512,512]{2,1,0:T(8,128)(2,1)} %get-tuple-element.105, s32[]{:T(128)} %get-tuple-element.104, s32[]{:T(128)} %get-tuple-element.112, s32[512]{0:T(512)S(1)} %add_multiply_fusion.2), kind=kLoop, calls=%fused_computation.25.clone.1 | loop fusion | flops 9175040 | bytes 527360 | tf_op jit(solution)/shard_map/while/body/jit(dynamic_update_index_in_dim)/dynamic_update_slice | solution.py:45
  53.1 0.6 add_multiply_fusion.2
  53.7 5.9 %fusion.29 = bf16[14,512,512]{2,1,0:T(8,128)(2,1)} fusion(bf16[14,512,512]{2,1,0:T(8,128)(2,1)} %get-tuple-element.105, s32[]{:T(128)} %get-tuple-element.104, s32[]{:T(128)} %get-tuple-element.112, s32[512]{0:T(512)S(1)} %add_multiply_fusion.2), kind=kLoop, calls=%fused_computation.25.clone.1 | loop fusion | flops 9175040 | bytes 527360 | tf_op jit(solution)/shard_map/while/body/jit(dynamic_update_index_in_dim)/dynamic_update_slice | solution.py:45
  60.2 0.6 add_multiply_fusion.2
  60.8 5.9 %fusion.29 = bf16[14,512,512]{2,1,0:T(8,128)(2,1)} fusion(bf16[14,512,512]{2,1,0:T(8,128)(2,1)} %get-tuple-element.105, s32[]{:T(128)} %get-tuple-element.104, s32[]{:T(128)} %get-tuple-element.112, s32[512]{0:T(512)S(1)} %add_multiply_fusion.2), kind=kLoop, calls=%fused_computation.25.clone.1 | loop fusion | flops 9175040 | bytes 527360 | tf_op jit(solution)/shard_map/while/body/jit(dynamic_update_index_in_dim)/dynamic_update_slice | solution.py:45
  67.3 0.6 add_multiply_fusion.2
  67.9 5.9 %fusion.29 = bf16[14,512,512]{2,1,0:T(8,128)(2,1)} fusion(bf16[14,512,512]{2,1,0:T(8,128)(2,1)} %get-tuple-element.105, s32[]{:T(128)} %get-tuple-element.104, s32[]{:T(128)} %get-tuple-element.112, s32[512]{0:T(512)S(1)} %add_multiply_fusion.2), kind=kLoop, calls=%fused_computation.25.clone.1 | loop fusion | flops 9175040 | bytes 527360 | tf_op jit(solution)/shard_map/while/body/jit(dynamic_update_index_in_dim)/dynamic_update_slice | solution.py:45
  75.0 5.9 %fusion.29 = bf16[14,512,512]{2,1,0:T(8,128)(2,1)} fusion(bf16[14,512,512]{2,1,0:T(8,128)(2,1)} %get-tuple-element.105, s32[]{:T(128)} %get-tuple-element.104, s32[]{:T(128)} %get-tuple-element.112, s32[512]{0:T(512)S(1)} %add_multiply_fusion.2), kind=kLoop, calls=%fused_computation.25.clone.1 | loop fusion | flops 9175040 | bytes 527360 | tf_op jit(solution)/shard_map/while/body/jit(dynamic_update_index_in_dim)/dynamic_update_slice | solution.py:45
  81.5 0.6 add_multiply_fusion.2
  82.1 5.9 %fusion.29 = bf16[14,512,512]{2,1,0:T(8,128)(2,1)} fusion(bf16[14,512,512]{2,1,0:T(8,128)(2,1)} %get-tuple-element.105, s32[]{:T(128)} %get-tuple-element.104, s32[]{:T(128)} %get-tuple-element.112, s32[512]{0:T(512)S(1)} %add_multiply_fusion.2), kind=kLoop, calls=%fused_computation.25.clone.1 | loop fusion | flops 9175040 | bytes 527360 | tf_op jit(solution)/shard_map/while/body/jit(dynamic_update_index_in_dim)/dynamic_update_slice | solution.py:45
  89.2 5.9 %fusion.29 = bf16[14,512,512]{2,1,0:T(8,128)(2,1)} fusion(bf16[14,512,512]{2,1,0:T(8,128)(2,1)} %get-tuple-element.105, s32[]{:T(128)} %get-tuple-element.104, s32[]{:T(128)} %get-tuple-element.112, s32[512]{0:T(512)S(1)} %add_multiply_fusion.2), kind=kLoop, calls=%fused_computation.25.clone.1 | loop fusion | flops 9175040 | bytes 527360 | tf_op jit(solution)/shard_map/while/body/jit(dynamic_update_index_in_dim)/dynamic_update_slice | solution.py:45
  96.3 5.9 %fusion.29 = bf16[14,512,512]{2,1,0:T(8,128)(2,1)} fusion(bf16[14,512,512]{2,1,0:T(8,128)(2,1)} %get-tuple-element.105, s32[]{:T(128)} %get-tuple-element.104, s32[]{:T(128)} %get-tuple-element.112, s32[512]{0:T(512)S(1)} %add_multiply_fusion.2), kind=kLoop, calls=%fused_computation.25.clone.1 | loop fusion | flops 9175040 | bytes 527360 | tf_op jit(solution)/shard_map/while/body/jit(dynamic_update_index_in_dim)/dynamic_update_slice | solution.py:45
  103.4 5.9 %fusion.29 = bf16[14,512,512]{2,1,0:T(8,128)(2,1)} fusion(bf16[14,512,512]{2,1,0:T(8,128)(2,1)} %get-tuple-element.105, s32[]{:T(128)} %get-tuple-element.104, s32[]{:T(128)} %get-tuple-element.112, s32[512]{0:T(512)S(1)} %add_multiply_fusion.2), kind=kLoop, calls=%fused_computation.25.clone.1 | loop fusion | flops 9175040 | bytes 527360 | tf_op jit(solution)/shard_map/while/body/jit(dynamic_update_index_in_dim)/dynamic_update_slice | solution.py:45
  109.3 5.2 %fusion.20 = f32[64,512]{1,0:T(8,128)} fusion(bf16[7168,512]{1,0:T(8,128)(2,1)} %bitcast.14, bf16[1,64,7168]{2,1,0:T(8,128)(2,1)S(1)} %copy-done), kind=kOutput, calls=%fused_computation.28 | convolution fusion | flops 469794816 | bytes 8388608 | tf_op jit(solution)/shard_map/dot_general | solution.py:47
  114.5 19.3 %reduce-scatter.2.cloned.1.call-done = f32[16,512]{1,0:T(8,128)} async-done(((f32[64,512]{1,0:T(8,128)}), f32[16,512]{1,0:T(8,128)}) %reduce-scatter.2.cloned.1.call-update) | async-done | bytes 32784 | tf_op jit(solution)/shard_map/reduce_scatter | solution.py:50
  133.8 3.0 %collective-permute-start = (f32[16,512]{1,0:T(8,128)}, f32[16,512]{1,0:T(8,128)S(1)}, u32[]{:S(2)}, u32[]{:S(2)}) collective-permute-start(f32[16,512]{1,0:T(8,128)} %reduce-scatter.2.cloned.1.call-done), channel_id=1, source_target_pairs={{0,8},{8,0},{16,24},{24,16},{1,9},{9,1},{17,25},{25,17},{2,10},{10... | collective-permute-start | bytes 98312 | tf_op jit(solution)/shard_map/ppermute | solution.py:54
  136.9 1.1 collective-permute-done
  137.9 0.8 add.96
  138.7 1.2 collective-permute-start.1
  140.6 0.9 collective-permute-done.1
  141.5 6.2 %multiply_divide_fusion = (f32[16,7168]{1,0:T(8,128)}, f32[16,7168]{1,0:T(8,128)}, f32[16,7168]{1,0:T(8,128)}) fusion(f32[]{:T(128)} %bitcast.6, f32[]{:T(128)} %bitcast.5, f32[16,7168]{1,0:T(8,128)S(1)} %copy-done.1, f32[16,7168]{1,0:T(8,128)S(1)} %copy-done.2, bf16[7168,512]{1,0:T(8,128)(2,1)} %bitcast.15, f32[16,512]{1,0:T(8,128)S(1)} %add.96, ...), kind=kOutput, calls=%fused_computation.32 | convolution fusion | flops 118718464 | bytes 9699336 | tf_op jit(solution)/shard_map/dot_general | solution.py:56
  (30 shorter events, 12.1 us)
Async XLA Ops:
  7.2 102.1 %copy-start = (bf16[1,64,7168]{2,1,0:T(8,128)(2,1)S(1)}, bf16[1,64,7168]{2,1,0:T(8,128)(2,1)}, u32[]{:S(2)}) copy-start(bf16[1,64,7168]{2,1,0:T(8,128)(2,1)} %param.7) | copy-start | bytes 2752516
  7.2 126.6 %reduce-scatter.2.cloned.1.call-start = ((), (), s32[]{:S(2)}) async-start(), calls=%async_computation.1 | async-start | bytes 163840 | tf_op jit(solution)/shard_map/reduce_scatter | solution.py:50
  109.3 32.2 %copy-start.1 = (f32[16,7168]{1,0:T(8,128)S(1)}, f32[16,7168]{1,0:T(8,128)}, u32[]{:S(2)}) copy-start(f32[16,7168]{1,0:T(8,128)} %param.11) | copy-start | bytes 1376260
  109.3 32.2 %copy-start.2 = (f32[16,7168]{1,0:T(8,128)S(1)}, f32[16,7168]{1,0:T(8,128)}, u32[]{:S(2)}) copy-start(f32[16,7168]{1,0:T(8,128)} %param.10) | copy-start | bytes 1376260
  133.8 4.1 %collective-permute-start = (f32[16,512]{1,0:T(8,128)}, f32[16,512]{1,0:T(8,128)S(1)}, u32[]{:S(2)}, u32[]{:S(2)}) collective-permute-start(f32[16,512]{1,0:T(8,128)} %reduce-scatter.2.cloned.1.call-done), channel_id=1, source_target_pairs={{0,8},{8,0},{16,24},{24,16},{1,9},{9,1},{17,25},{25,17},{2,10},{10... | collective-permute-start | bytes 98312 | tf_op jit(solution)/shard_map/ppermute | solution.py:54
  138.7 2.8 %collective-permute-start.1 = (f32[16,512]{1,0:T(8,128)S(1)}, f32[16,512]{1,0:T(8,128)S(1)}, u32[]{:S(2)}, u32[]{:S(2)}) collective-permute-start(f32[16,512]{1,0:T(8,128)S(1)} %add.96), channel_id=1, source_target_pairs={{0,16},{8,24},{16,0},{24,8},{1,17},{9,25},{17,1},{25,9},{2,18},{10... | collective-permute-start | bytes 98312 | tf_op jit(solution)/shard_map/ppermute | solution.py:54
Sparse Core Ops, SparseCore 0:
  114.6 19.1 reduce-scatter.1
